TPU v7x, 512 devices: a whole 4x8x8 slice. The times are simulated.
512 devices in a mesh: req: 64 (over x, z, core), ch: 8 (over y).
Axes of the slice: x: 4, y: 8, z: 8, core: 2. Of those that a mesh axis runs over, the one named last changes fastest.
Arguments:
- tokens: bfloat16 [128, 4096], P('req', 'ch'), may hold values from -80 to 80
- attn_gain: float32 [4096], P('ch'), may hold values from 0.1 to 1.9
- w_query: bfloat16 [4096, 4096], P('ch', 'req'), may hold values from -0.09375 to 0.09375
- w_keyval: bfloat16 [4096, 512], P('ch', 'req'), may hold values from -0.09375 to 0.09375
- cache: bfloat16 [2, 128, 256, 2048], P(None, 'req', 'ch'), may hold values from -70 to 70
- lengths: int32 [128], P('req'), may hold values from 1 to 2047, as said below
- write_pos: int32 [128], P('req'), may hold values from 0 to 2047
- w_out: bfloat16 [4096, 4096], P('ch', 'req'), may hold values from -0.09375 to 0.09375
- mlp_gain: float32 [4096], P('ch'), may hold values from 0.1 to 1.9
- w_gate_up: bfloat16 [4096, 24576], P('ch', 'req'), may hold values from -0.09375 to 0.09375
- w_down: bfloat16 [12288, 4096], P('req', 'ch'), may hold values from -0.0546875 to 0.0546875
Outputs:
- layer_out: bfloat16 [128, 4096], P('req', 'ch')
- kv_new: bfloat16 [128, 512], P('req', 'ch')
Inputs may be any that keep to these rules, and one draw needn't show every extreme that they name: lengths[b] earlier tokens of request b are in the cache; the largest equals 2047 in every draw. The new token of request b goes to slot write_pos[b]; its earlier tokens fill the slots before it, going back cyclically.
All inputs are finite; a program needn't handle non-finite values.
Results may differ from a plain program's by a relative error of at most 0.0064.
Values may be sent and summed in bfloat16 or wider, within the bound.
No kernel may reach another device: no remote copies, remote signals or barrier semaphores. Data moves between devices by JAX's collectives and lax.ppermute only.
A program may use at most 64 MiB of HBM per device.

v0:
```python
import math
import jax
import jax.numpy as jnp
from jax import lax
from jax.sharding import PartitionSpec as P

D = 4096
H = 16
HD = 256
EPSILON = 1e-06


def rms_norm(values, gain):
    wide = values.astype(jnp.float32)
    squares = jnp.sum(wide * wide, axis=1)
    summed = lax.psum(squares, "ch")
    meansq = summed / D
    return (wide * lax.rsqrt(meansq + EPSILON)[:, None] * gain[None, :]).astype(jnp.bfloat16)


def body(
    tokens,
    attn_gain,
    w_query,
    w_keyval,
    cache,
    lengths,
    write_pos,
    w_out,
    mlp_gain,
    w_gate_up,
    w_down,
):
    rows = tokens.shape[0]
    chan = cache.shape[2]
    window = cache.shape[3]
    factor = 1.0 / math.sqrt(HD)
    normed = rms_norm(tokens, attn_gain)
    joined = jnp.concatenate([w_query, w_keyval], axis=1)
    head_parts = jnp.dot(
        lax.all_gather(normed, "req", axis=0, tiled=True),
        joined,
        preferred_element_type=jnp.float32,
    )
    query_cols = w_query.shape[1]
    query_part, keyval_part = (
        lax.all_to_all(head_parts[:, :query_cols], "req", split_axis=0, concat_axis=1, tiled=True),
        lax.all_to_all(head_parts[:, query_cols:], "req", split_axis=0, concat_axis=1, tiled=True),
    )
    query_sum, keyval_sum = (
        lax.psum_scatter(query_part, "ch", scatter_dimension=1, tiled=True),
        lax.psum_scatter(keyval_part, "ch", scatter_dimension=1, tiled=True),
    )
    queries = query_sum.astype(jnp.bfloat16).reshape(rows, H, chan)
    keyval_new = keyval_sum.astype(jnp.bfloat16)
    key_new = keyval_new[:, :chan]
    value_new = keyval_new[:, chan:]
    keys = cache[0]
    values_cache = cache[1]
    own_part = jnp.sum(
        queries.astype(jnp.float32) * key_new.astype(jnp.float32)[:, None, :], axis=-1
    )
    score_part = jnp.einsum("bhe,bew->bhw", queries, keys, preferred_element_type=jnp.float32)
    summed, own_sum = lax.psum((score_part, own_part), "ch")
    slot_index = jnp.arange(window, dtype=jnp.int32)
    offset = (write_pos[:, None] - 1 - slot_index[None, :]) % window
    usable = offset < lengths[:, None]
    scores = jnp.where(usable[:, None, :], summed * factor, -jnp.inf)
    own_score = own_sum * factor
    top = jnp.maximum(jnp.max(scores, axis=-1), own_score)
    weights = jnp.exp(scores - top[..., None])
    own_weight = jnp.exp(own_score - top)
    total = jnp.sum(weights, axis=-1) + own_weight
    weights_low = weights.astype(jnp.bfloat16)
    numer = jnp.einsum(
        "bhw,bew->bhe", weights_low, values_cache, preferred_element_type=jnp.float32
    )
    numer = (
        numer
        + own_weight.astype(jnp.bfloat16).astype(jnp.float32)[..., None]
        * value_new.astype(jnp.float32)[:, None, :]
    )
    attn_local = (numer / total[..., None]).astype(jnp.bfloat16).reshape(rows, H * chan)
    out_parts = jnp.dot(
        lax.all_gather(attn_local, "req", axis=0, tiled=True),
        w_out,
        preferred_element_type=jnp.float32,
    )
    out_part = lax.all_to_all(out_parts, "req", split_axis=0, concat_axis=1, tiled=True)
    out_sum = lax.psum_scatter(out_part, "ch", scatter_dimension=1, tiled=True)
    first = (tokens.astype(jnp.float32) + out_sum).astype(jnp.bfloat16)
    normed_two = rms_norm(first, mlp_gain)
    hidden_cols = w_gate_up.shape[1] // 2
    ffn_parts = jnp.dot(
        lax.all_gather(normed_two, "req", axis=0, tiled=True),
        w_gate_up,
        preferred_element_type=jnp.float32,
    )
    ffn_total = lax.psum(ffn_parts, "ch")
    hidden = (
        jax.nn.gelu(ffn_total[:, :hidden_cols], approximate=True) * ffn_total[:, hidden_cols:]
    ).astype(jnp.bfloat16)
    down_sum = lax.psum_scatter(
        jnp.dot(hidden, w_down, preferred_element_type=jnp.float32),
        "req",
        scatter_dimension=0,
        tiled=True,
    )
    layer_out = (first.astype(jnp.float32) + down_sum).astype(jnp.bfloat16)
    return (layer_out, keyval_new)


def solution(mesh):
    placed = (
        P("req", "ch"),
        P("ch"),
        P("ch", "req"),
        P("ch", "req"),
        P(None, "req", "ch", None),
        P("req"),
        P("req"),
        P("ch", "req"),
        P("ch"),
        P("ch", "req"),
        P("req", "ch"),
    )
    return jax.shard_map(
        body,
        mesh=mesh,
        in_specs=placed,
        out_specs=(P("req", "ch"), P("req", "ch")),
        check_vma=False,
    )
```

profile of v0, /device:TPU:1, one launch (start us, length us, event | category | flops | bytes accessed | tf_op | source)
XLA Modules:
  0.0 728.1 jit_solution(11447148937282177522)
XLA Ops:
  7.2 0.8 fusion.36
  8.0 14.7 %psum.35 = f32[2]{0:T(128)S(1)} all-reduce(f32[2]{0:T(128)S(1)} %fusion.36), channel_id=1, replica_groups=mesh['req'=64,'ch'=8] {'ch'}, use_global_device_ids=true, to_apply=%region_1.0 | all-reduce | flops 2 | bytes 16 | tf_op jit(solution)/shard_map/psum | solution.py:16
  22.7 0.8 fusion.45
  23.5 60.2 %all-gather = bf16[64,2,512]{2,1,0:T(2,128)(2,1)S(1)} all-gather(bf16[1,2,512]{2,1,0:T(2,128)(2,1)S(1)} %fusion.45), channel_id=1, replica_groups=mesh['req'=64,'ch'=8] {'req'}, dimensions={0}, use_global_device_ids=true | all-gather | bytes 133120 | tf_op jit(solution)/shard_map/all_gather | solution.py:41
  83.7 0.1 reshape.72
  83.7 1.0 fusion.24
  84.8 0.7 copy.28
  85.5 5.6 all-to-all-start.1
  91.1 0.1 copy.26
  91.2 0.7 reshape.85
  91.9 8.9 %all-to-all-done.1 = f32[64,2,8]{2,1,0:T(2,128)S(1)} async-done(((f32[64,2,8]{2,1,0:T(2,128)}), f32[64,2,8]{2,1,0:T(2,128)S(1)}, u32[]{:S(2)}, u32[]{:S(2)}) %all-to-all-start.1) | async-done | bytes 4128 | tf_op jit(solution)/shard_map/all_to_all | solution.py:48
  100.8 4.4 all-to-all-start
  105.2 0.0 reduce-scatter.12.cloned.1.call-start
  105.2 1.2 copy.40
  106.4 0.0 reduce-scatter.12.cloned.1.call-update
  106.4 0.0 reduce-scatter.10.cloned.1.call-start
  106.5 0.7 broadcast_add_fusion
  107.2 7.5 %all-to-all-done = f32[64,1,128]{2,1,0:T(1,128)S(1)} async-done(((f32[64,1,128]{2,1,0:T(1,128)}), f32[64,1,128]{2,1,0:T(1,128)S(1)}, u32[]{:S(2)}, u32[]{:S(2)}) %all-to-all-start) | async-done | bytes 32800 | tf_op jit(solution)/shard_map/all_to_all | solution.py:47
  114.6 0.5 broadcast.73
  115.1 0.7 reduce
  115.9 0.1 reshape.86
  116.0 2.0 copy.39
  118.0 0.0 reduce-scatter.10.cloned.1.call-update
  118.1 0.0 all-reduce.5.cloned.1.call-start
  118.1 0.1 fusion.35
  118.2 23.1 %reduce-scatter.12.cloned.1.call-done = f32[64,2]{1,0:T(8,128)} async-done(((f32[512,2]{1,0:T(8,128)}), f32[64,2]{1,0:T(8,128)}) %reduce-scatter.12.cloned.1.call-update) | async-done | bytes 528
  141.3 0.8 copy.36
  142.2 47.1 %reduce-scatter.10.cloned.1.call-done = f32[512,2]{1,0:T(8,128)} async-done(((f32[4096,2]{1,0:T(8,128)}), f32[512,2]{1,0:T(8,128)}) %reduce-scatter.10.cloned.1.call-update) | async-done | bytes 4112
  189.3 1.1 copy.34
  190.4 0.1 reshape.69
  190.5 0.9 fusion.3
  191.4 0.0 reduce-scatter.14.cloned.1.call-start
  191.4 0.1 slice_convert_fusion
  191.5 0.1 multiply_reduce_fusion
  191.6 11.9 %psum.37 = f32[2,16]{1,0:T(2,128)S(1)} all-reduce(f32[2,16]{1,0:T(2,128)S(1)} %multiply_reduce_fusion), channel_id=1, replica_groups=mesh['req'=64,'ch'=8] {'ch'}, use_global_device_ids=true, to_apply=%region_7.8 | all-reduce | flops 32 | bytes 256 | tf_op jit(solution)/shard_map/psum | solution.py:64
  203.5 64.4 %all-reduce.5.cloned.1.call-done = f32[2,16,2048]{2,1,0:T(8,128)} async-done(((f32[2,16,2048]{2,1,0:T(8,128)}), f32[2,16,2048]{2,1,0:T(8,128)}) %all-reduce.5.cloned.1.call-update) | async-done | bytes 262160 | tf_op jit(solution)/shard_map/psum | solution.py:64
  267.9 1.1 fusion.7
  269.0 1.2 fusion.8
  270.1 1.2 fusion.1
  271.4 0.1 reshape.73
  271.4 57.0 %all-gather.1 = bf16[64,2,512]{2,1,0:T(2,128)(2,1)S(1)} all-gather(bf16[1,2,512]{2,1,0:T(2,128)(2,1)S(1)} %reshape.73), channel_id=1, replica_groups=mesh['req'=64,'ch'=8] {'req'}, dimensions={0}, use_global_device_ids=true | all-gather | bytes 133120 | tf_op jit(solution)/shard_map/all_gather | solution.py:85
  328.4 0.1 reshape.74
  328.5 0.2 fusion.55
  328.7 0.1 reshape.87
  328.8 16.1 %all_to_all.57 = f32[64,1,128]{2,1,0:T(1,128)S(1)} all-to-all(f32[64,1,128]{2,1,0:T(1,128)S(1)} %reshape.87), channel_id=1, replica_groups=mesh['req'=64,'ch'=8] {'req'}, dimensions={0} | all-to-all | bytes 65536 | tf_op jit(solution)/shard_map/all_to_all | solution.py:89
  344.9 0.7 reduce.1
  345.6 0.1 reshape.88
  345.8 2.0 copy.41
  347.8 0.0 reduce-scatter.14.cloned.1.call-update
  347.8 0.0 all-reduce.7.cloned.1.call-start
  347.9 32.4 %reduce-scatter.14.cloned.1.call-done = f32[512,2]{1,0:T(8,128)} async-done(((f32[4096,2]{1,0:T(8,128)}), f32[512,2]{1,0:T(8,128)}) %reduce-scatter.14.cloned.1.call-update) | async-done | bytes 4112
  380.3 1.1 copy.38
  381.4 0.1 fusion.40
  381.5 12.0 %psum.38 = f32[2]{0:T(128)S(1)} all-reduce(f32[2]{0:T(128)S(1)} %get-tuple-element.2), channel_id=1, replica_groups=mesh['req'=64,'ch'=8] {'ch'}, use_global_device_ids=true, to_apply=%region_11.12 | all-reduce | flops 2 | bytes 16 | tf_op jit(solution)/shard_map/psum | solution.py:16
  393.5 0.1 fusion.44
  393.6 59.6 %all-gather.2 = bf16[64,2,512]{2,1,0:T(2,128)(2,1)S(1)} all-gather(bf16[1,2,512]{2,1,0:T(2,128)(2,1)S(1)} %fusion.44), channel_id=1, replica_groups=mesh['req'=64,'ch'=8] {'req'}, dimensions={0}, use_global_device_ids=true | all-gather | bytes 133120 | tf_op jit(solution)/shard_map/all_gather | solution.py:95
  453.2 0.1 reshape.76
  453.2 0.9 fusion.56
  454.2 0.0 all-reduce.9.cloned.1.call-start
  454.2 69.2 %all-reduce.7.cloned.1.call-done = f32[128,384]{1,0:T(8,128)} async-done(((f32[128,384]{1,0:T(8,128)}), f32[128,384]{1,0:T(8,128)}) %all-reduce.7.cloned.1.call-update) | async-done | bytes 196624 | tf_op jit(solution)/shard_map/psum | solution.py:99
  523.4 1.9 fusion.28
  525.3 1.3 dynamic-slice
  527.3 192.7 %all-reduce.9.cloned.1.call-done = f32[128,512]{1,0:T(8,128)} async-done(((f32[128,512]{1,0:T(8,128)}), f32[128,512]{1,0:T(8,128)}) %all-reduce.9.cloned.1.call-update) | async-done | bytes 262160
  720.0 1.3 fusion.43
  (25 shorter events, 0.1 us)
Async XLA Ops:
  7.2 446.1 %copy-start = (bf16[512,384]{1,0:T(8,128)(2,1)S(1)}, bf16[512,384]{1,0:T(8,128)(2,1)}, u32[]{:S(2)}) copy-start(bf16[512,384]{1,0:T(8,128)(2,1)} %param.20) | copy-start | bytes 1179652
  85.5 15.3 %all-to-all-start.1 = ((f32[64,2,8]{2,1,0:T(2,128)}), f32[64,2,8]{2,1,0:T(2,128)S(1)}, u32[]{:S(2)}, u32[]{:S(2)}) async-start(f32[64,2,8]{2,1,0:T(2,128)} %bitcast.4), calls=%async_computation.1 | async-start | bytes 131072 | tf_op jit(solution)/shard_map/all_to_all | solution.py:48
  100.8 13.8 %all-to-all-start = ((f32[64,1,128]{2,1,0:T(1,128)}), f32[64,1,128]{2,1,0:T(1,128)S(1)}, u32[]{:S(2)}, u32[]{:S(2)}) async-start(f32[64,1,128]{2,1,0:T(1,128)} %reshape.85), calls=%async_computation | async-start | bytes 65536 | tf_op jit(solution)/shard_map/all_to_all | solution.py:47
  105.2 36.1 %reduce-scatter.12.cloned.1.call-start = ((), (), s32[]{:S(2)}) async-start(), calls=%async_computation.9 | async-start | bytes 294912
  106.4 82.9 %reduce-scatter.10.cloned.1.call-start = ((), (), s32[]{:S(2)}) async-start(), calls=%async_computation.8 | async-start | bytes 2359296
  116.0 2.2 copy-start.7
  116.0 74.5 %copy-start.2 = (bf16[2,2,32,2048]{3,2,1,0:T(8,128)(2,1)S(1)}, bf16[2,2,32,2048]{3,2,1,0:T(8,128)(2,1)}, u32[]{:S(2)}) copy-start(bf16[2,2,32,2048]{3,2,1,0:T(8,128)(2,1)} %param.15) | copy-start | bytes 1572868
  118.0 210.5 %copy-start.3 = (bf16[512,64]{0,1:T(8,128)(2,1)S(1)}, bf16[512,64]{0,1:T(8,128)(2,1)}, u32[]{:S(2)}) copy-start(bf16[512,64]{0,1:T(8,128)(2,1)} %param.18) | copy-start | bytes 196612
  118.1 149.8 %all-reduce.5.cloned.1.call-start = ((), (), s32[]{:S(2)}) async-start(), calls=%async_computation.6 | async-start | bytes 524288 | tf_op jit(solution)/shard_map/psum | solution.py:64
  142.2 205.6 %copy-start.5 = (bf16[2,64]{1,0:T(2,128)(2,1)}, bf16[2,64]{1,0:T(2,128)(2,1)S(1)}, u32[]{:S(2)}) copy-start(bf16[2,64]{1,0:T(2,128)(2,1)S(1)} %copy.36) | copy-start | bytes 772
  191.4 188.9 %reduce-scatter.14.cloned.1.call-start = ((), (), s32[]{:S(2)}) async-start(), calls=%async_computation.10 | async-start | bytes 2359296
  345.7 35.6 %copy-start.4 = (bf16[2,512]{1,0:T(2,128)(2,1)S(1)}, bf16[2,512]{1,0:T(2,128)(2,1)}, u32[]{:S(2)}) copy-start(bf16[2,512]{1,0:T(2,128)(2,1)} %param.11) | copy-start | bytes 6148
  345.8 47.8 %copy-start.6 = (f32[512]{0:T(512)S(1)}, f32[512]{0:T(512)}, u32[]{:S(2)}) copy-start(f32[512]{0:T(512)} %param.19) | copy-start | bytes 6148
  347.8 175.6 %copy-start.1 = (bf16[192,512]{1,0:T(8,128)(2,1)S(1)}, bf16[192,512]{1,0:T(8,128)(2,1)}, u32[]{:S(2)}) copy-start(bf16[192,512]{1,0:T(8,128)(2,1)} %param.21) | copy-start | bytes 589828
  347.8 175.6 %all-reduce.7.cloned.1.call-start = ((), (), s32[]{:S(2)}) async-start(), calls=%async_computation.7 | async-start | bytes 393216 | tf_op jit(solution)/shard_map/psum | solution.py:99
  454.2 265.8 %all-reduce.9.cloned.1.call-start = ((), (), s32[]{:S(2)}) async-start(), calls=%async_computation.11 | async-start | bytes 524288
Sparse Core Ops, SparseCore 0:
  108.8 32.4 reduce-scatter.11
  144.2 45.0 reduce-scatter.9
  191.6 76.2 all-reduce.4
  348.0 32.2 reduce-scatter.13
  454.3 69.0 all-reduce.6
  526.7 193.2 all-reduce.8
where the time goes:
time: 729 us; the launch traced here: 728 us
  waiting for transfers between devices  446 us (61%)
  blocking collectives  231 us (32%)
  between operations  15 us (2%)
  local copies, waits for them, and re-layouts  12.2 us (2%)
  starting transfers between devices  10.2 us (1%)
  other arithmetic  7.74 us (1%)
    unnamed x10, waiting for transfers between devices  295 us
    psum x1, waiting for transfers between devices, body(): ffn_total = lax.psum(ffn_parts, 'ch')  69.2 us
    psum x1, waiting for transfers between devices, body(): summed, own_sum = lax.psum((score_part, own_part), 'ch')  64.4 us
    all_gather x1, blocking collectives, body(): lax.all_gather(normed, 'req', axis=0, tiled=True)  60.2 us
    all_gather x1, blocking collectives, body(): lax.all_gather(normed_two, 'req', axis=0, tiled=True)  59.6 us
    all_gather x1, blocking collectives, body(): lax.all_gather(attn_local, 'req', axis=0, tiled=True)  57 us
    psum x2, blocking collectives, rms_norm(): summed = lax.psum(squares, 'ch')  26.7 us
    all_to_all x1, blocking collectives, body(): lax.all_to_all(out_parts, 'req', split_axis=0, concat_axis=1, tiled=True)  16.1 us
  transfers between devices with their start and end apart: 8, of which 8 were waited for; matrix products, arithmetic and copies ran while one was open for 1% of the time, Pallas kernels for 0%

commit v1 on v0

--- a/solution.py
+++ b/solution.py
@@ -8,6 +8,14 @@
 H = 16
 HD = 256
 EPSILON = 1e-06
+
+
+def sum_by_hops(value, axis):
+    size, total = (lax.axis_size(axis), value)
+    for reach in [1 << k for k in range(size.bit_length() - 1)]:
+        swap = [(i, i ^ reach) for i in range(size)]
+        total = total + lax.ppermute(total, axis, swap)
+    return total
 
 
 def rms_norm(values, gain):
@@ -96,7 +104,7 @@
         w_gate_up,
         preferred_element_type=jnp.float32,
     )
-    ffn_total = lax.psum(ffn_parts, "ch")
+    ffn_total = sum_by_hops(ffn_parts, "ch")
     hidden = (
         jax.nn.gelu(ffn_total[:, :hidden_cols], approximate=True) * ffn_total[:, hidden_cols:]
     ).astype(jnp.bfloat16)

time: 729 us -> 686 us (0.941)
  waiting for transfers between devices: 446 us -> 392 us
  starting transfers between devices: 10.2 us -> 22 us
    psum x1 -> x0, waiting for transfers between devices: 69.2 us -> none  [body(): ffn_total = lax.psum(ffn_parts, 'ch')]
    ppermute x0 -> x3, waiting for transfers between devices: none -> 24.7 us  [sum_by_hops(): total = total + lax.ppermute(total, axis, swap)]
    ppermute x0 -> x3, starting transfers between devices: none -> 11.9 us  [sum_by_hops(): total = total + lax.ppermute(total, axis, swap)]
    unnamed x10 -> x9, waiting for transfers between devices: 295 us -> 287 us
  transfers between devices with their start and end apart: 8 -> 10, of which waited for: 8 -> 10; matrix products, arithmetic and copies ran while one was open for 1% -> 1% of each run, Pallas kernels for 0% -> 0%
where the time goes in v1:
time: 686 us; the launch traced here: 685 us
  waiting for transfers between devices  392 us (57%)
  blocking collectives  231 us (34%)
  starting transfers between devices  22 us (3%)
  between operations  14.7 us (2%)
  local copies, waits for them, and re-layouts  12.2 us (2%)
  other arithmetic  7.81 us (1%)
    unnamed x9, waiting for transfers between devices  287 us
    psum x1, waiting for transfers between devices, body(): summed, own_sum = lax.psum((score_part, own_part), 'ch')  64.4 us
    all_gather x1, blocking collectives, body(): lax.all_gather(normed, 'req', axis=0, tiled=True)  60.2 us
    all_gather x1, blocking collectives, body(): lax.all_gather(normed_two, 'req', axis=0, tiled=True)  59.6 us
    all_gather x1, blocking collectives, body(): lax.all_gather(attn_local, 'req', axis=0, tiled=True)  57 us
    psum x2, blocking collectives, rms_norm(): summed = lax.psum(squares, 'ch')  26.7 us
    ppermute x3, waiting for transfers between devices, sum_by_hops(): total = total + lax.ppermute(total, axis, swap)  24.7 us
    all_to_all x1, blocking collectives, body(): lax.all_to_all(out_parts, 'req', split_axis=0, concat_axis=1, tiled=True)  16.1 us
  transfers between devices with their start and end apart: 10, of which 10 were waited for; matrix products, arithmetic and copies ran while one was open for 1% of the time, Pallas kernels for 0%

profile of v1, /device:TPU:1, one launch (start us, length us, event | category | flops | bytes accessed | tf_op | source)
XLA Modules:
  0.0 685.1 jit_solution(15757812545150767217)
XLA Ops:
  7.2 0.8 fusion.36
  8.0 14.7 %psum.28 = f32[2]{0:T(128)S(1)} all-reduce(f32[2]{0:T(128)S(1)} %fusion.36), channel_id=1, replica_groups=mesh['req'=64,'ch'=8] {'ch'}, use_global_device_ids=true, to_apply=%region_1.0 | all-reduce | flops 2 | bytes 16 | tf_op jit(solution)/shard_map/psum | solution.py:24
  22.7 0.8 fusion.45
  23.5 60.2 %all-gather = bf16[64,2,512]{2,1,0:T(2,128)(2,1)S(1)} all-gather(bf16[1,2,512]{2,1,0:T(2,128)(2,1)S(1)} %fusion.45), channel_id=1, replica_groups=mesh['req'=64,'ch'=8] {'req'}, dimensions={0}, use_global_device_ids=true | all-gather | bytes 133120 | tf_op jit(solution)/shard_map/all_gather | solution.py:49
  83.7 0.1 reshape.72
  83.7 1.0 fusion.24
  84.8 0.7 copy.28
  85.5 5.6 all-to-all-start.1
  91.1 0.1 copy.26
  91.2 0.7 reshape.85
  91.9 8.9 %all-to-all-done.1 = f32[64,2,8]{2,1,0:T(2,128)S(1)} async-done(((f32[64,2,8]{2,1,0:T(2,128)}), f32[64,2,8]{2,1,0:T(2,128)S(1)}, u32[]{:S(2)}, u32[]{:S(2)}) %all-to-all-start.1) | async-done | bytes 4128 | tf_op jit(solution)/shard_map/all_to_all | solution.py:56
  100.8 4.4 all-to-all-start
  105.2 0.0 reduce-scatter.12.cloned.1.call-start
  105.2 1.2 copy.40
  106.4 0.0 reduce-scatter.10.cloned.1.call-start
  106.5 0.7 broadcast_add_fusion
  107.2 7.5 %all-to-all-done = f32[64,1,128]{2,1,0:T(1,128)S(1)} async-done(((f32[64,1,128]{2,1,0:T(1,128)}), f32[64,1,128]{2,1,0:T(1,128)S(1)}, u32[]{:S(2)}, u32[]{:S(2)}) %all-to-all-start) | async-done | bytes 32800 | tf_op jit(solution)/shard_map/all_to_all | solution.py:55
  114.6 0.5 broadcast.73
  115.1 0.7 reduce
  115.9 0.1 reshape.86
  116.0 2.0 copy.39
  118.1 0.0 all-reduce.4.cloned.1.call-start
  118.1 0.1 fusion.35
  118.2 23.1 %reduce-scatter.12.cloned.1.call-done = f32[64,2]{1,0:T(8,128)} async-done(((f32[512,2]{1,0:T(8,128)}), f32[64,2]{1,0:T(8,128)}) %reduce-scatter.12.cloned.1.call-update) | async-done | bytes 528
  141.3 0.8 copy.36
  142.2 47.1 %reduce-scatter.10.cloned.1.call-done = f32[512,2]{1,0:T(8,128)} async-done(((f32[4096,2]{1,0:T(8,128)}), f32[512,2]{1,0:T(8,128)}) %reduce-scatter.10.cloned.1.call-update) | async-done | bytes 4112
  189.3 1.1 copy.34
  190.4 0.1 reshape.69
  190.5 0.9 fusion.3
  191.4 0.0 reduce-scatter.14.cloned.1.call-start
  191.4 0.1 slice_convert_fusion
  191.5 0.1 multiply_reduce_fusion
  191.6 11.9 %psum.30 = f32[2,16]{1,0:T(2,128)S(1)} all-reduce(f32[2,16]{1,0:T(2,128)S(1)} %multiply_reduce_fusion), channel_id=1, replica_groups=mesh['req'=64,'ch'=8] {'ch'}, use_global_device_ids=true, to_apply=%region_7.8 | all-reduce | flops 32 | bytes 256 | tf_op jit(solution)/shard_map/psum | solution.py:72
  203.5 64.4 %all-reduce.4.cloned.1.call-done = f32[2,16,2048]{2,1,0:T(8,128)} async-done(((f32[2,16,2048]{2,1,0:T(8,128)}), f32[2,16,2048]{2,1,0:T(8,128)}) %all-reduce.4.cloned.1.call-update) | async-done | bytes 262160 | tf_op jit(solution)/shard_map/psum | solution.py:72
  267.9 1.1 fusion.7
  269.0 1.2 fusion.8
  270.1 1.2 fusion.1
  271.4 0.1 reshape.73
  271.4 57.0 %all-gather.1 = bf16[64,2,512]{2,1,0:T(2,128)(2,1)S(1)} all-gather(bf16[1,2,512]{2,1,0:T(2,128)(2,1)S(1)} %reshape.73), channel_id=1, replica_groups=mesh['req'=64,'ch'=8] {'req'}, dimensions={0}, use_global_device_ids=true | all-gather | bytes 133120 | tf_op jit(solution)/shard_map/all_gather | solution.py:93
  328.4 0.1 reshape.74
  328.5 0.2 fusion.55
  328.7 0.1 reshape.87
  328.8 16.1 %all_to_all.57 = f32[64,1,128]{2,1,0:T(1,128)S(1)} all-to-all(f32[64,1,128]{2,1,0:T(1,128)S(1)} %reshape.87), channel_id=1, replica_groups=mesh['req'=64,'ch'=8] {'req'}, dimensions={0} | all-to-all | bytes 65536 | tf_op jit(solution)/shard_map/all_to_all | solution.py:97
  344.9 0.7 reduce.1
  345.6 0.1 reshape.88
  345.8 2.0 copy.41
  347.9 32.4 %reduce-scatter.14.cloned.1.call-done = f32[512,2]{1,0:T(8,128)} async-done(((f32[4096,2]{1,0:T(8,128)}), f32[512,2]{1,0:T(8,128)}) %reduce-scatter.14.cloned.1.call-update) | async-done | bytes 4112
  380.3 1.1 copy.38
  381.4 0.1 fusion.40
  381.5 12.0 %psum.31 = f32[2]{0:T(128)S(1)} all-reduce(f32[2]{0:T(128)S(1)} %get-tuple-element.2), channel_id=1, replica_groups=mesh['req'=64,'ch'=8] {'ch'}, use_global_device_ids=true, to_apply=%region_11.12 | all-reduce | flops 2 | bytes 16 | tf_op jit(solution)/shard_map/psum | solution.py:24
  393.5 0.1 fusion.44
  393.6 59.6 %all-gather.2 = bf16[64,2,512]{2,1,0:T(2,128)(2,1)S(1)} all-gather(bf16[1,2,512]{2,1,0:T(2,128)(2,1)S(1)} %fusion.44), channel_id=1, replica_groups=mesh['req'=64,'ch'=8] {'req'}, dimensions={0}, use_global_device_ids=true | all-gather | bytes 133120 | tf_op jit(solution)/shard_map/all_gather | solution.py:103
  453.2 0.1 reshape.76
  453.2 0.2 fusion.56
  453.5 2.5 collective-permute-start
  456.0 5.7 collective-permute-done
  461.7 2.9 collective-permute-start.1
  464.6 10.6 %collective-permute-done.1 = f32[128,384]{1,0:T(8,128)S(1)} collective-permute-done((f32[128,384]{1,0:T(8,128)S(1)}, f32[128,384]{1,0:T(8,128)S(1)}, u32[]{:S(2)}, u32[]{:S(2)}) %collective-permute-start.1) | collective-permute-done | bytes 196640 | tf_op jit(solution)/shard_map/ppermute | solution.py:17
  475.2 6.5 collective-permute-start.2
  481.8 8.4 %collective-permute-done.2 = f32[128,384]{1,0:T(8,128)S(1)} collective-permute-done((f32[128,384]{1,0:T(8,128)S(1)}, f32[128,384]{1,0:T(8,128)S(1)}, u32[]{:S(2)}, u32[]{:S(2)}) %collective-permute-start.2) | collective-permute-done | bytes 196640 | tf_op jit(solution)/shard_map/ppermute | solution.py:17
  490.2 0.9 fusion.28
  491.2 1.3 dynamic-slice
  493.1 184.2 %all-reduce.6.cloned.1.call-done = f32[128,512]{1,0:T(8,128)} async-done(((f32[128,512]{1,0:T(8,128)}), f32[128,512]{1,0:T(8,128)}) %all-reduce.6.cloned.1.call-update) | async-done | bytes 262160
  677.3 1.3 fusion.43
  (31 shorter events, 0.3 us)
Async XLA Ops:
  7.2 446.1 %copy-start = (bf16[512,384]{1,0:T(8,128)(2,1)S(1)}, bf16[512,384]{1,0:T(8,128)(2,1)}, u32[]{:S(2)}) copy-start(bf16[512,384]{1,0:T(8,128)(2,1)} %param.20) | copy-start | bytes 1179652
  85.5 15.3 %all-to-all-start.1 = ((f32[64,2,8]{2,1,0:T(2,128)}), f32[64,2,8]{2,1,0:T(2,128)S(1)}, u32[]{:S(2)}, u32[]{:S(2)}) async-start(f32[64,2,8]{2,1,0:T(2,128)} %bitcast.4), calls=%async_computation.1 | async-start | bytes 131072 | tf_op jit(solution)/shard_map/all_to_all | solution.py:56
  100.8 13.8 %all-to-all-start = ((f32[64,1,128]{2,1,0:T(1,128)}), f32[64,1,128]{2,1,0:T(1,128)S(1)}, u32[]{:S(2)}, u32[]{:S(2)}) async-start(f32[64,1,128]{2,1,0:T(1,128)} %reshape.85), calls=%async_computation | async-start | bytes 65536 | tf_op jit(solution)/shard_map/all_to_all | solution.py:55
  105.2 36.1 %reduce-scatter.12.cloned.1.call-start = ((), (), s32[]{:S(2)}) async-start(), calls=%async_computation.8 | async-start | bytes 294912
  106.4 82.9 %reduce-scatter.10.cloned.1.call-start = ((), (), s32[]{:S(2)}) async-start(), calls=%async_computation.7 | async-start | bytes 2359296
  116.0 2.2 copy-start.7
  116.0 74.5 %copy-start.2 = (bf16[2,2,32,2048]{3,2,1,0:T(8,128)(2,1)S(1)}, bf16[2,2,32,2048]{3,2,1,0:T(8,128)(2,1)}, u32[]{:S(2)}) copy-start(bf16[2,2,32,2048]{3,2,1,0:T(8,128)(2,1)} %param.15) | copy-start | bytes 1572868
  118.0 210.5 %copy-start.3 = (bf16[512,64]{0,1:T(8,128)(2,1)S(1)}, bf16[512,64]{0,1:T(8,128)(2,1)}, u32[]{:S(2)}) copy-start(bf16[512,64]{0,1:T(8,128)(2,1)} %param.18) | copy-start | bytes 196612
  118.1 149.8 %all-reduce.4.cloned.1.call-start = ((), (), s32[]{:S(2)}) async-start(), calls=%async_computation.6 | async-start | bytes 524288 | tf_op jit(solution)/shard_map/psum | solution.py:72
  142.2 205.6 %copy-start.5 = (bf16[2,64]{1,0:T(2,128)(2,1)}, bf16[2,64]{1,0:T(2,128)(2,1)S(1)}, u32[]{:S(2)}) copy-start(bf16[2,64]{1,0:T(2,128)(2,1)S(1)} %copy.36) | copy-start | bytes 772
  191.4 188.9 %reduce-scatter.14.cloned.1.call-start = ((), (), s32[]{:S(2)}) async-start(), calls=%async_computation.9 | async-start | bytes 2359296
  345.7 35.6 %copy-start.4 = (bf16[2,512]{1,0:T(2,128)(2,1)S(1)}, bf16[2,512]{1,0:T(2,128)(2,1)}, u32[]{:S(2)}) copy-start(bf16[2,512]{1,0:T(2,128)(2,1)} %param.11) | copy-start | bytes 6148
  345.8 47.8 %copy-start.6 = (f32[512]{0:T(512)S(1)}, f32[512]{0:T(512)}, u32[]{:S(2)}) copy-start(f32[512]{0:T(512)} %param.19) | copy-start | bytes 6148
  347.8 142.4 %copy-start.1 = (bf16[192,512]{1,0:T(8,128)(2,1)S(1)}, bf16[192,512]{1,0:T(8,128)(2,1)}, u32[]{:S(2)}) copy-start(bf16[192,512]{1,0:T(8,128)(2,1)} %param.21) | copy-start | bytes 589828
  347.9 329.4 %all-reduce.6.cloned.1.call-start = ((), (), s32[]{:S(2)}) async-start(), calls=%async_computation.10 | async-start | bytes 524288
  453.5 8.2 %collective-permute-start = (f32[128,384]{1,0:T(8,128)S(1)}, f32[128,384]{1,0:T(8,128)S(1)}, u32[]{:S(2)}, u32[]{:S(2)}) collective-permute-start(f32[128,384]{1,0:T(8,128)S(1)} %fusion.56), channel_id=1, source_target_pairs={{0,1},{1,0},{2,3},{3,2},{4,5},{5,4},{6,7},{7,6},{8,9},{9,8},{10,11... | collective-permute-start | bytes 589832 | tf_op jit(solution)/shard_map/ppermute | solution.py:17
  461.7 13.5 %collective-permute-start.1 = (f32[128,384]{1,0:T(8,128)S(1)}, f32[128,384]{1,0:T(8,128)S(1)}, u32[]{:S(2)}, u32[]{:S(2)}) collective-permute-start(f32[128,384]{1,0:T(8,128)S(1)} %add.70), channel_id=1, source_target_pairs={{0,2},{1,3},{2,0},{3,1},{4,6},{5,7},{6,4},{7,5},{8,10},{9,11},{10,... | collective-permute-start | bytes 589832 | tf_op jit(solution)/shard_map/ppermute | solution.py:17
  475.2 15.0 %collective-permute-start.2 = (f32[128,384]{1,0:T(8,128)S(1)}, f32[128,384]{1,0:T(8,128)S(1)}, u32[]{:S(2)}, u32[]{:S(2)}) collective-permute-start(f32[128,384]{1,0:T(8,128)S(1)} %add.71), channel_id=1, source_target_pairs={{0,4},{1,5},{2,6},{3,7},{4,0},{5,1},{6,2},{7,3},{8,12},{9,13},{10,... | collective-permute-start | bytes 589832 | tf_op jit(solution)/shard_map/ppermute | solution.py:17
Sparse Core Ops, SparseCore 0:
  108.8 32.4 reduce-scatter.11
  144.2 45.0 reduce-scatter.9
  191.6 76.2 all-reduce.3
  348.0 32.2 reduce-scatter.13
  491.3 185.9 all-reduce.5
